TPU v7x, 256 devices: a whole 4x4x8 slice. The times are simulated.
256 devices in a mesh: grp: 32 (over y, z_lo, core), tp: 8 (over x, z_hi).
Axes of the slice: x: 4, y: 4, z: 8 (z_hi: 2, z_lo: 4; z = z_hi * 4 + z_lo), core: 2. Of those that a mesh axis runs over, the one named last changes fastest.
Arguments:
- tok_ids: int32 [8192], P('grp'), may hold values from 0 to 16383
- accept: int32 [8192], P('grp'), may hold values 0 or 1
- sub_ids: int32 [8192], P('grp'), may hold values from 0 to 16383
- cache_len: int32 [32], replicated, may hold values from 256 to 3840, as said below
- spill: int32 [32], replicated, may hold values from 0 to 1792, as said below
- embed: bfloat16 [16384, 2048], P('grp', 'tp'), may hold values from -6 to 6
- attn_gain: float32 [2048], replicated, may hold values from 0.25 to 1.75
- w_query: bfloat16 [2048, 2048], P(None, 'tp'), may hold values from -0.125 to 0.125
- w_key: bfloat16 [2048, 512], P(None, 'tp'), as said below
- w_value: bfloat16 [2048, 512], P(None, 'tp'), as said below
- w_out: bfloat16 [2048, 2048], P('tp'), may hold values from -2.5 to 2.5
- mlp_gain: float32 [2048], replicated, may hold values from 0.25 to 1.75
- w_gate: bfloat16 [2048, 5632], P(None, 'tp'), may hold values from -0.125 to 0.125
- w_up: bfloat16 [2048, 5632], P(None, 'tp'), may hold values from -0.125 to 0.125
- w_down: bfloat16 [5632, 2048], P('tp'), may hold values from -0.078125 to 0.078125
- cache_keys: bfloat16 [65536, 512], P('grp', 'tp'), may hold values from -320 to 320, as said below
- cache_values: bfloat16 [65536, 512], P('grp', 'tp'), may hold values from -8 to 8, as said below
Outputs:
- first_out: bfloat16 [8192, 2048], P('grp', 'tp')
- second_out: bfloat16 [8192, 2048], P('grp', 'tp')
Inputs may be any that keep to these rules, and one draw needn't show every extreme that they name: Request g keeps cache_len[g] - spill[g] >= 256 positions in slots from 0 of store g and spill[g] positions in the last slots of store (g xor 1); for every g, cache_len[g] - spill[g] + spill[g xor 1] <= 2048. Of each pair of groups 2k, 2k + 1 at most one has spill above 0. `w_key`: the 2 stored copies of a key-value head are equal. `w_value`: the 2 stored copies of a key-value head are equal. `cache_keys`: the 2 stored copies of a key-value head are equal. `cache_values`: the 2 stored copies of a key-value head are equal.
All inputs are finite; a program needn't handle non-finite values. No bound on the sum of `accept` on one device may be relied on, other than what follows from the above.
Results may differ from a plain program's by a relative error of at most 0.024.
Values may be sent and summed in bfloat16 or wider, within the bound.
No kernel may reach another device: no remote copies, remote signals or barrier semaphores. Data moves between devices by JAX's collectives and lax.ppermute only.
A program may use at most 128 MiB of HBM per device.

v0:
```python
import jax
import jax.numpy as jnp
from jax import lax
from jax.sharding import PartitionSpec as P

HD = 64
EPSILON = 1e-05
SENTINEL = -1e30


def swapped(array, axis, bit):
    return lax.ppermute(array, axis, [(i, i ^ 1 << bit) for i in range(lax.axis_size(axis))])


def rms_normed(values, gain):
    square = jnp.mean(values * values, axis=-1, keepdims=True)
    return (values * lax.rsqrt(square + EPSILON) * gain).astype(jnp.bfloat16)


def rotate(vectors, positions):
    half = vectors.shape[-1] // 2
    exponent = jnp.arange(half, dtype=jnp.float32) * (-2.0 / vectors.shape[-1])
    freqs = jnp.power(jnp.float32(10000.0), exponent)
    angles = positions.astype(jnp.float32)[:, None] * freqs[None, :]
    cosine = jnp.cos(angles)[:, None, :]
    sine = jnp.sin(angles)[:, None, :]
    first = vectors[..., :half]
    second = vectors[..., half:]
    return jnp.concatenate(
        [first * cosine - second * sine, second * cosine + first * sine], axis=-1
    )


def partial_attention(query, keys, values, valid):
    scores = jnp.einsum("bcgd,kcd->bcgk", query, keys, preferred_element_type=jnp.float32) * 0.125
    scores = jnp.where(valid, scores, SENTINEL)
    top = jnp.max(scores, axis=-1)
    weights = jnp.where(valid, jnp.exp(scores - top[..., None]), 0.0)
    total = jnp.sum(weights, axis=-1)
    weighted = jnp.einsum(
        "bcgk,kcd->bcgd", weights.astype(jnp.bfloat16), values, preferred_element_type=jnp.float32
    )
    return (weighted, top, total)


def on_device(
    tok_ids,
    accept,
    sub_ids,
    cache_len,
    spill,
    embed,
    attn_gain,
    w_query,
    w_key,
    w_value,
    w_out,
    mlp_gain,
    w_gate,
    w_up,
    w_down,
    cache_keys,
    cache_values,
):
    block = tok_ids.shape[0]
    slots = cache_keys.shape[0]
    local_vocab = embed.shape[0]
    query_local = w_query.shape[1] // HD
    stored_local = w_key.shape[1] // HD
    per_stored = query_local // stored_local
    group_index = lax.axis_index("grp")
    shard_index = lax.axis_index("tp")
    own_count = cache_len[group_index] - spill[group_index]
    far_count = spill[group_index]
    positions = cache_len[group_index] + jnp.arange(block, dtype=jnp.int32)
    slot_ids = jnp.arange(slots, dtype=jnp.int32)
    tail_ids = slot_ids[block:]
    store_keys = cache_keys.reshape(slots, stored_local, HD)
    store_values = cache_values.reshape(slots, stored_local, HD)
    block_valid = jnp.ones((block,), dtype=bool)
    second_ids = jnp.where(accept == 1, sub_ids, tok_ids)
    vocab_base = group_index * local_vocab
    vocab_ids = jnp.arange(local_vocab, dtype=jnp.int32)

    def lookup(id_list):
        onehot = (id_list[:, None] - vocab_base == vocab_ids[None, :]).astype(jnp.bfloat16)
        return jnp.dot(onehot, embed, preferred_element_type=jnp.float32)

    all_first, all_second = (
        lax.all_gather(tok_ids, "grp", axis=0, tiled=True),
        lax.all_gather(second_ids, "grp", axis=0, tiled=True),
    )
    first_rows = lax.psum_scatter(
        lookup(all_first).astype(jnp.bfloat16), "grp", scatter_dimension=0, tiled=True
    )
    second_rows = lax.psum_scatter(
        lookup(all_second).astype(jnp.bfloat16), "grp", scatter_dimension=0, tiled=True
    )
    tail_keys, tail_values = swapped((cache_keys[block:], cache_values[block:]), "grp", 0)
    far_keys = tail_keys.reshape(slots - block, stored_local, HD)
    far_values = tail_values.reshape(slots - block, stored_local, HD)
    far_valid = tail_ids >= slots - far_count

    def denoise(x_part):
        width = x_part.shape[1]
        x_full = lax.all_gather(x_part, "tp", axis=1, tiled=True)
        normed = rms_normed(x_full.astype(jnp.float32), attn_gain)
        query = rotate(
            jnp.dot(normed, w_query, preferred_element_type=jnp.float32).reshape(
                block, query_local, HD
            ),
            positions,
        )
        query = query.astype(jnp.bfloat16).reshape(block, stored_local, per_stored, HD)
        new_keys = rotate(
            jnp.dot(normed, w_key, preferred_element_type=jnp.float32).reshape(
                block, stored_local, HD
            ),
            positions,
        ).astype(jnp.bfloat16)
        new_values = (
            jnp.dot(normed, w_value, preferred_element_type=jnp.float32)
            .reshape(block, stored_local, HD)
            .astype(jnp.bfloat16)
        )
        own_valid = slot_ids < own_count
        keys = jnp.concatenate([store_keys, far_keys, new_keys], axis=0)
        values = jnp.concatenate([store_values, far_values, new_values], axis=0)
        valid = jnp.concatenate([own_valid, far_valid, block_valid])
        weighted, top, total = partial_attention(query, keys, values, valid)
        attended = weighted / total[..., None]
        mixed = attended.reshape(block, query_local * HD).astype(jnp.bfloat16)
        head_term = jnp.dot(mixed, w_out, preferred_element_type=jnp.float32)
        head_sum = lax.psum(head_term.astype(jnp.bfloat16), "tp").astype(jnp.float32)
        resid_full = (x_full.astype(jnp.float32) + head_sum).astype(jnp.bfloat16)
        resid_part = lax.dynamic_slice_in_dim(resid_full, shard_index * width, width, 1)
        normed_mlp = rms_normed(resid_full.astype(jnp.float32), mlp_gain)
        gate = jnp.dot(normed_mlp, w_gate, preferred_element_type=jnp.float32)
        lift = jnp.dot(normed_mlp, w_up, preferred_element_type=jnp.float32)
        hidden = (jax.nn.silu(gate) * lift).astype(jnp.bfloat16)
        down_term = jnp.dot(hidden, w_down, preferred_element_type=jnp.float32)
        down_part = lax.psum_scatter(
            down_term.astype(jnp.bfloat16), "tp", scatter_dimension=1, tiled=True
        ).astype(jnp.float32)
        return (resid_part.astype(jnp.float32) + down_part).astype(jnp.bfloat16)

    return (denoise(first_rows), denoise(second_rows))


def solution(mesh):
    placed = (
        P("grp"),
        P("grp"),
        P("grp"),
        P(),
        P(),
        P("grp", "tp"),
        P(),
        P(None, "tp"),
        P(None, "tp"),
        P(None, "tp"),
        P("tp", None),
        P(),
        P(None, "tp"),
        P(None, "tp"),
        P("tp", None),
        P("grp", "tp"),
        P("grp", "tp"),
    )
    return jax.shard_map(
        on_device,
        mesh=mesh,
        in_specs=placed,
        out_specs=(P("grp", "tp"), P("grp", "tp")),
        check_vma=False,
    )
```

profile of v0, /device:TPU:8, one launch (start us, length us, event | category | flops | bytes accessed | tf_op | source)
XLA Modules:
  0.0 960.8 jit_solution(10995285730689573226)
XLA Ops:
  8.1 37.6 %all-gather.1 = s32[32,1,256]{2,1,0:T(1,128)S(1)} all-gather(s32[1,1,256]{2,1,0:T(1,128)S(1)} %bitcast.193), channel_id=1, replica_groups=mesh['grp'=32,'tp'=8] {'grp'}, dimensions={0}, use_global_device_ids=true | all-gather | bytes 33792 | tf_op jit(solution)/shard_map/all_gather | solution.py:91
  45.7 38.2 %all-gather = s32[32,1,256]{2,1,0:T(1,128)S(1)} all-gather(s32[1,1,256]{2,1,0:T(1,128)} %bitcast.192), channel_id=1, replica_groups=mesh['grp'=32,'tp'=8] {'grp'}, dimensions={0}, use_global_device_ids=true | all-gather | bytes 33792 | tf_op jit(solution)/shard_map/all_gather | solution.py:90
  83.9 6.3 fusion.10
  91.1 5.4 fusion.11
  96.6 131.9 %reduce-scatter.9.cloned.1.call-done = bf16[256,256]{1,0:T(8,128)(2,1)} async-done(((bf16[8192,256]{1,0:T(8,128)(2,1)}), bf16[256,256]{1,0:T(8,128)(2,1)}) %reduce-scatter.9.cloned.1.call-update) | async-done | bytes 131088 | tf_op jit(solution)/shard_map/reduce_scatter | solution.py:96
  228.6 151.1 %reduce-scatter.5.cloned.1.call-done = bf16[256,256]{1,0:T(8,128)(2,1)} async-done(((bf16[8192,256]{1,0:T(8,128)(2,1)}), bf16[256,256]{1,0:T(8,128)(2,1)}) %reduce-scatter.5.cloned.1.call-update) | async-done | bytes 131088 | tf_op jit(solution)/shard_map/reduce_scatter | solution.py:93
  386.7 73.9 %all-gather.7.cloned.1.call-done = bf16[256,2048]{1,0:T(8,128)(2,1)} async-done(((bf16[256,256]{1,0:T(8,128)(2,1)}), bf16[256,2048]{1,0:T(8,128)(2,1)}) %all-gather.7.cloned.1.call-update) | async-done | bytes 1048592 | tf_op jit(solution)/shard_map/all_gather | solution.py:106
  462.1 58.2 %all-gather.5.cloned.1.call-done = bf16[256,2048]{1,0:T(8,128)(2,1)} async-done(((bf16[256,256]{1,0:T(8,128)(2,1)}), bf16[256,2048]{1,0:T(8,128)(2,1)}) %all-gather.5.cloned.1.call-update) | async-done | bytes 1048592 | tf_op jit(solution)/shard_map/all_gather | solution.py:106
  520.3 1.7 fusion.30
  522.0 2.3 fusion.114
  526.3 8.1 fusion.61
  534.5 14.5 %bitcast_reduce_fusion = (f32[256,4]{0,1:T(4,128)S(1)}, f32[256,4]{0,1:T(4,128)S(1)}, f32[4096,256,4]{1,0,2:T(8,128)}) fusion(pred[4096]{0:T(1024)(128)(4,1)S(1)} %pad_add_fusion, f32[4096,256,4]{1,0,2:T(8,128)} %fusion.61, bf16[256,4,32]{0,2,1:T(8,128)(2,1)S(1)} %get-tuple-element.13, bf16[256,4,32]{0,2,1:T(8,128)(2,1)S(1)} %get-tuple-element.12, ...), kind=kOutput, calls=%fused_computation.1 | convolution fusion | flops 564393984 | bytes 34222080 | tf_op jit(solution)/shard_map/bcgd,kcd->bcgk/dot_general | solution.py:35
  549.0 14.2 %fusion.8 = (f32[256,4]{0,1:T(4,128)S(1)}, f32[256,4]{0,1:T(4,128)S(1)}) fusion(f32[4096,256,4]{1,0,2:T(8,128)} %get-tuple-element.26, f32[256,4]{0,1:T(4,128)S(1)} %get-tuple-element.4, pred[4096]{0:T(1024)(128)(4,1)S(1)} %pad_add_fusion, f32[256,4]{0,1:T(4,128)S(1)} %get-tuple-element.5, f32[4096,256,4]{1,0,2:T(8,128)} %fusion.61), kind=kLoop, calls=%fused_computation.16 | loop fusion | flops 41940992 | bytes 33574912 | tf_op jit(solution)/shard_map/reduce_sum | solution.py:39
  563.8 5.4 fusion.51
  571.3 5.1 fusion.57
  578.2 190.4 %all-reduce.3.cloned.1.call-done = (bf16[256,2048]{1,0:T(8,128)(2,1)}, bf16[256,2048]{1,0:T(8,128)(2,1)}) async-done(((bf16[256,2048]{1,0:T(8,128)(2,1)}, bf16[256,2048]{1,0:T(8,128)(2,1)}), (bf16[256,2048]{1,0:T(8,128)(2,1)}, bf16[256,2048]{1,0:T(8,128)(2,1)})) %all-reduce.3.cloned.1.call-update) | async-done | bytes 2097168 | tf_op jit(solution)/shard_map/psum | solution.py:134
  768.6 2.2 fusion.24
  771.8 1.9 fusion.78
  773.8 6.6 convolution_convert_fusion.2
  780.5 2.2 fusion.27
  783.7 1.9 fusion.74
  785.6 6.6 convolution_convert_fusion
  792.3 72.7 %reduce-scatter.7.cloned.1.call-done = bf16[256,256]{1,0:T(8,128)(2,1)} async-done(((bf16[256,2048]{1,0:T(8,128)(2,1)}), bf16[256,256]{1,0:T(8,128)(2,1)}) %reduce-scatter.7.cloned.1.call-update) | async-done | bytes 131088 | tf_op jit(solution)/shard_map/reduce_scatter | solution.py:142
  866.6 85.6 %reduce-scatter.11.cloned.1.call-done = bf16[256,256]{1,0:T(8,128)(2,1)} async-done(((bf16[256,2048]{1,0:T(8,128)(2,1)}), bf16[256,256]{1,0:T(8,128)(2,1)}) %reduce-scatter.11.cloned.1.call-update) | async-done | bytes 131088 | tf_op jit(solution)/shard_map/reduce_scatter | solution.py:142
  (101 shorter events, 20.1 us)
Async XLA Ops:
  7.2 766.6 %copy-start = (bf16[704,2048]{1,0:T(8,128)(2,1)S(1)}, bf16[704,2048]{1,0:T(8,128)(2,1)}, u32[]{:S(2)}) copy-start(bf16[704,2048]{1,0:T(8,128)(2,1)} %param.31) | copy-start | bytes 8650756
  7.2 221.3 %reduce-scatter.9.cloned.1.call-start = ((), (), s32[]{:S(2)}) async-start(), calls=%async_computation.7 | async-start | bytes 4325376 | tf_op jit(solution)/shard_map/reduce_scatter | solution.py:96
  90.2 289.5 %reduce-scatter.5.cloned.1.call-start = ((), (), s32[]{:S(2)}) async-start(), calls=%async_computation.4 | async-start | bytes 4325376 | tf_op jit(solution)/shard_map/reduce_scatter | solution.py:93
  96.5 283.2 %copy-start.6 = (bf16[2048,64]{0,1:T(8,128)(2,1)S(1)}, bf16[2048,64]{0,1:T(8,128)(2,1)}, u32[]{:S(2)}) copy-start(bf16[2048,64]{0,1:T(8,128)(2,1)} %param.32) | copy-start | bytes 786436
  96.5 286.1 %copy-start.16 = (s32[32]{0:T(128)S(1)}, s32[32]{0:T(128)}, u32[]{:S(2)}) copy-start(s32[32]{0:T(128)} %param.20) | copy-start | bytes 388
  96.5 286.7 %copy-start.17 = (s32[32]{0:T(128)S(1)}, s32[32]{0:T(128)}, u32[]{:S(2)}) copy-start(s32[32]{0:T(128)} %param.21) | copy-start | bytes 388
  96.5 425.4 %copy-start.14 = (f32[2048]{0:T(1024)S(1)}, f32[2048]{0:T(1024)}, u32[]{:S(2)}) copy-start(f32[2048]{0:T(1024)} %param.23) | copy-start | bytes 24580
  96.6 364.0 %all-gather.7.cloned.1.call-start = ((), (), s32[]{:S(2)}) async-start(), calls=%async_computation.8 | async-start | bytes 1179648 | tf_op jit(solution)/shard_map/all_gather | solution.py:106
  228.5 291.7 %all-gather.5.cloned.1.call-start = ((), (), s32[]{:S(2)}) async-start(), calls=%async_computation.5 | async-start | bytes 1179648 | tf_op jit(solution)/shard_map/all_gather | solution.py:106
  379.7 388.9 %all-reduce.3.cloned.1.call-start = ((), (), s32[]{:S(2)}) async-start(), calls=%async_computation.10 | async-start | bytes 4194304 | tf_op jit(solution)/shard_map/psum | solution.py:134
  380.5 145.9 %collective-permute-start.1 = (bf16[1792,64]{0,1:T(8,128)(2,1)}, bf16[1792,64]{0,1:T(8,128)(2,1)S(1)}, u32[]{:S(2)}, u32[]{:S(2)}) collective-permute-start(bf16[1792,64]{0,1:T(8,128)(2,1)} %slice.35), channel_id=1, source_target_pairs={{0,8},{8,0},{16,24},{24,16},{32,40},{40,32},{48,56},{56,48},{64,72... | collective-permute-start | bytes 688136 | tf_op jit(solution)/shard_map/ppermute | solution.py:12
  382.1 181.6 %collective-permute-start = (bf16[1792,64]{0,1:T(8,128)(2,1)}, bf16[1792,64]{0,1:T(8,128)(2,1)}, u32[]{:S(2)}, u32[]{:S(2)}) collective-permute-start(bf16[1792,64]{0,1:T(8,128)(2,1)} %slice.33), channel_id=1, source_target_pairs={{0,8},{8,0},{16,24},{24,16},{32,40},{40,32},{48,56},{56,48},{64,72... | collective-permute-start | bytes 688136 | tf_op jit(solution)/shard_map/ppermute | solution.py:12
  534.5 29.3 %slice-start = ((s8[16777216]{0:T(1024)(128)(4,1)}), s8[4194304]{0:T(1024)(128)(4,1)S(1)}, s32[]{:S(2)}) async-start(s8[16777216]{0:T(1024)(128)(4,1)} %bitcast.174), calls=%async_computation.11 | async-start | bytes 8388608
  534.5 29.3 %slice-start.1 = ((s8[16777216]{0:T(1024)(128)(4,1)}), s8[4194304]{0:T(1024)(128)(4,1)S(1)}, s32[]{:S(2)}) async-start(s8[16777216]{0:T(1024)(128)(4,1)} %bitcast.174), calls=%async_computation.12 | async-start | bytes 8388608
  534.5 29.3 %slice-start.2 = ((s8[16777216]{0:T(1024)(128)(4,1)}), s8[4194304]{0:T(1024)(128)(4,1)S(1)}, s32[]{:S(2)}) async-start(s8[16777216]{0:T(1024)(128)(4,1)} %bitcast.174), calls=%async_computation.13 | async-start | bytes 8388608
  549.0 14.2 %copy-start.13 = (bf16[2048,64]{0,1:T(8,128)(2,1)S(1)}, bf16[2048,64]{0,1:T(8,128)(2,1)}, u32[]{:S(2)}) copy-start(bf16[2048,64]{0,1:T(8,128)(2,1)} %param.26) | copy-start | bytes 786436
  549.0 14.8 %slice-start.3 = ((s8[16777216]{0:T(1024)(128)(4,1)}), s8[4194304]{0:T(1024)(128)(4,1)S(1)}, s32[]{:S(2)}) async-start(s8[16777216]{0:T(1024)(128)(4,1)} %bitcast.174), calls=%async_computation.14 | async-start | bytes 8388608
  549.0 14.8 %copy-start.7 = (bf16[2048,64]{0,1:T(8,128)(2,1)S(1)}, bf16[2048,64]{0,1:T(8,128)(2,1)}, u32[]{:S(2)}) copy-start(bf16[2048,64]{0,1:T(8,128)(2,1)} %param.33) | copy-start | bytes 786436
  563.2 8.1 slice-start.4
  563.8 7.5 slice-start.5
  563.8 7.5 slice-start.6
  577.9 194.0 %copy-start.15 = (f32[2048]{0:T(1024)S(1)}, f32[2048]{0:T(1024)}, u32[]{:S(2)}) copy-start(f32[2048]{0:T(1024)} %param.28) | copy-start | bytes 24580
  577.9 287.1 %reduce-scatter.7.cloned.1.call-start = ((), (), s32[]{:S(2)}) async-start(), calls=%async_computation.6 | async-start | bytes 1179648 | tf_op jit(solution)/shard_map/reduce_scatter | solution.py:142
  780.5 171.8 %reduce-scatter.11.cloned.1.call-start = ((), (), s32[]{:S(2)}) async-start(), calls=%async_computation.9 | async-start | bytes 1179648 | tf_op jit(solution)/shard_map/reduce_scatter | solution.py:142
  (11 other events, 36.6 us)
Sparse Core Ops, SparseCore 0:
  90.3 138.1 reduce-scatter.8
  231.0 148.6 reduce-scatter.4
  382.2 78.3 all-gather.6
  462.9 57.3 all-gather.4
  578.0 190.5 all-reduce.2
  780.6 84.3 reduce-scatter.6
  869.4 82.7 reduce-scatter.10
where the time goes:
time: 961 us
  waiting for transfers between devices  764 us (80%)
  blocking collectives  75.8 us (8%)
  matrix products  70 us (7%)
  other arithmetic  27.1 us (3%)
  between operations  16.5 us (2%)
    psum x1, waiting for transfers between devices, denoise(): lax.psum(head_term.astype(jnp.bfloat16), 'tp').astype(jnp.float32)  190 us
    reduce_scatter x2, waiting for transfers between devices, denoise(): lax.psum_scatter(down_term.astype(jnp.bfloat16), 'tp', scatter_dimension=...  158 us
    reduce_scatter x1, waiting for transfers between devices, on_device(): lax.psum_scatter(lookup(all_first).astype(jnp.bfloat16), 'grp', scatter_d...  151 us
    all_gather x2, waiting for transfers between devices, denoise(): x_full = lax.all_gather(x_part, 'tp', axis=1, tiled=True)  132 us
    reduce_scatter x1, waiting for transfers between devices, on_device(): lax.psum_scatter(lookup(all_second).astype(jnp.bfloat16), 'grp', scatter_...  132 us
    all_gather x1, blocking collectives, on_device(): lax.all_gather(tok_ids, 'grp', axis=0, tiled=True)  38.2 us
    all_gather x1, blocking collectives, on_device(): lax.all_gather(second_ids, 'grp', axis=0, tiled=True)  37.6 us
    dot_general x2, matrix products, partial_attention(): jnp.einsum('bcgd,kcd->bcgk', query, keys, preferred_element_type=jnp.floa...  22.6 us
  transfers between devices with their start and end apart: 9, of which 7 were waited for; matrix products, arithmetic and copies ran while one was open for 7% of the time, Pallas kernels for 0%

commit v1 on v0

--- a/solution.py
+++ b/solution.py
@@ -86,8 +86,14 @@
         onehot = (id_list[:, None] - vocab_base == vocab_ids[None, :]).astype(jnp.bfloat16)
         return jnp.dot(onehot, embed, preferred_element_type=jnp.float32)
 
+    def run_records_over_axis(state):
+        outer = lax.axis_size("grp")
+        taken_in = jnp.stack([state] * outer, 0)
+        local_out = lax.all_to_all(taken_in, "grp", 0, 0)
+        return jnp.concatenate(local_out, 0)
+
     all_first, all_second = (
-        lax.all_gather(tok_ids, "grp", axis=0, tiled=True),
+        run_records_over_axis(tok_ids),
         lax.all_gather(second_ids, "grp", axis=0, tiled=True),
     )
     first_rows = lax.psum_scatter(

time: 961 us -> 932 us (0.970)
  blocking collectives: 75.8 us -> 36.1 us
    all_gather x1 -> x0, blocking collectives: 38.2 us -> none  [on_device(): lax.all_gather(tok_ids, 'grp', axis=0, tiled=True)]
  transfers between devices with their start and end apart: 9 -> 10, of which waited for: 7 -> 7; matrix products, arithmetic and copies ran while one was open for 7% -> 7% of each run, Pallas kernels for 0% -> 0%
where the time goes in v1:
time: 932 us; the launch traced here: 931 us
  waiting for transfers between devices  764 us (82%)
  matrix products  70 us (8%)
  blocking collectives  36.1 us (4%)
  other arithmetic  27 us (3%)
  between operations  16.5 us (2%)
  starting transfers between devices  10.2 us (1%)
    psum x1, waiting for transfers between devices, denoise(): lax.psum(head_term.astype(jnp.bfloat16), 'tp').astype(jnp.float32)  190 us
    reduce_scatter x2, waiting for transfers between devices, denoise(): lax.psum_scatter(down_term.astype(jnp.bfloat16), 'tp', scatter_dimension=...  158 us
    reduce_scatter x1, waiting for transfers between devices, on_device(): lax.psum_scatter(lookup(all_first).astype(jnp.bfloat16), 'grp', scatter_d...  152 us
    all_gather x2, waiting for transfers between devices, denoise(): x_full = lax.all_gather(x_part, 'tp', axis=1, tiled=True)  131 us
    reduce_scatter x1, waiting for transfers between devices, on_device(): lax.psum_scatter(lookup(all_second).astype(jnp.bfloat16), 'grp', scatter_...  131 us
    all_gather x1, blocking collectives, on_device(): lax.all_gather(second_ids, 'grp', axis=0, tiled=True)  36.1 us
    dot_general x2, matrix products, partial_attention(): jnp.einsum('bcgd,kcd->bcgk', query, keys, preferred_element_type=jnp.floa...  22.7 us
  transfers between devices with their start and end apart: 10, of which 7 were waited for; matrix products, arithmetic and copies ran while one was open for 7% of the time, Pallas kernels for 0%

profile of v1, /device:TPU:8, one launch (start us, length us, event | category | flops | bytes accessed | tf_op | source)
XLA Modules:
  0.0 931.3 jit_solution(10961414832630257322)
XLA Ops:
  8.6 9.1 all-to-all-start
  18.6 36.1 %all-gather = s32[32,1,256]{2,1,0:T(1,128)S(1)} all-gather(s32[1,1,256]{2,1,0:T(1,128)S(1)} %bitcast.191), channel_id=1, replica_groups=mesh['grp'=32,'tp'=8] {'grp'}, dimensions={0}, use_global_device_ids=true | all-gather | bytes 33792 | tf_op jit(solution)/shard_map/all_gather | solution.py:97
  54.7 6.3 fusion.10
  61.9 5.4 fusion.11
  67.5 131.0 %reduce-scatter.9.cloned.1.call-done = bf16[256,256]{1,0:T(8,128)(2,1)} async-done(((bf16[8192,256]{1,0:T(8,128)(2,1)}), bf16[256,256]{1,0:T(8,128)(2,1)}) %reduce-scatter.9.cloned.1.call-update) | async-done | bytes 131088 | tf_op jit(solution)/shard_map/reduce_scatter | solution.py:102
  198.6 152.3 %reduce-scatter.5.cloned.1.call-done = bf16[256,256]{1,0:T(8,128)(2,1)} async-done(((bf16[8192,256]{1,0:T(8,128)(2,1)}), bf16[256,256]{1,0:T(8,128)(2,1)}) %reduce-scatter.5.cloned.1.call-update) | async-done | bytes 131088 | tf_op jit(solution)/shard_map/reduce_scatter | solution.py:99
  357.8 73.1 %all-gather.6.cloned.1.call-done = bf16[256,2048]{1,0:T(8,128)(2,1)} async-done(((bf16[256,256]{1,0:T(8,128)(2,1)}), bf16[256,2048]{1,0:T(8,128)(2,1)}) %all-gather.6.cloned.1.call-update) | async-done | bytes 1048592 | tf_op jit(solution)/shard_map/all_gather | solution.py:112
  432.5 58.2 %all-gather.4.cloned.1.call-done = bf16[256,2048]{1,0:T(8,128)(2,1)} async-done(((bf16[256,256]{1,0:T(8,128)(2,1)}), bf16[256,2048]{1,0:T(8,128)(2,1)}) %all-gather.4.cloned.1.call-update) | async-done | bytes 1048592 | tf_op jit(solution)/shard_map/all_gather | solution.py:112
  490.6 1.7 fusion.30
  492.3 2.3 fusion.114
  496.7 8.1 fusion.61
  504.9 14.5 %bitcast_reduce_fusion = (f32[256,4]{0,1:T(4,128)S(1)}, f32[256,4]{0,1:T(4,128)S(1)}, f32[4096,256,4]{1,0,2:T(8,128)}) fusion(pred[4096]{0:T(1024)(128)(4,1)S(1)} %pad_add_fusion, f32[4096,256,4]{1,0,2:T(8,128)} %fusion.61, bf16[256,4,32]{0,2,1:T(8,128)(2,1)S(1)} %get-tuple-element.13, bf16[256,4,32]{0,2,1:T(8,128)(2,1)S(1)} %get-tuple-element.12, ...), kind=kOutput, calls=%fused_computation.1 | convolution fusion | flops 564393984 | bytes 34222080 | tf_op jit(solution)/shard_map/bcgd,kcd->bcgk/dot_general | solution.py:35
  519.4 14.2 %fusion.8 = (f32[256,4]{0,1:T(4,128)S(1)}, f32[256,4]{0,1:T(4,128)S(1)}) fusion(f32[4096,256,4]{1,0,2:T(8,128)} %get-tuple-element.26, f32[256,4]{0,1:T(4,128)S(1)} %get-tuple-element.4, pred[4096]{0:T(1024)(128)(4,1)S(1)} %pad_add_fusion, f32[256,4]{0,1:T(4,128)S(1)} %get-tuple-element.5, f32[4096,256,4]{1,0,2:T(8,128)} %fusion.61), kind=kLoop, calls=%fused_computation.16 | loop fusion | flops 41940992 | bytes 33574912 | tf_op jit(solution)/shard_map/reduce_sum | solution.py:39
  534.2 5.4 fusion.51
  541.7 5.1 fusion.57
  548.6 190.4 %all-reduce.3.cloned.1.call-done = (bf16[256,2048]{1,0:T(8,128)(2,1)}, bf16[256,2048]{1,0:T(8,128)(2,1)}) async-done(((bf16[256,2048]{1,0:T(8,128)(2,1)}, bf16[256,2048]{1,0:T(8,128)(2,1)}), (bf16[256,2048]{1,0:T(8,128)(2,1)}, bf16[256,2048]{1,0:T(8,128)(2,1)})) %all-reduce.3.cloned.1.call-update) | async-done | bytes 2097168 | tf_op jit(solution)/shard_map/psum | solution.py:140
  739.0 2.2 fusion.24
  742.2 1.9 fusion.78
  744.2 6.6 convolution_convert_fusion.2
  750.9 2.2 fusion.27
  754.1 1.9 fusion.74
  756.0 6.6 convolution_convert_fusion
  762.7 72.8 %reduce-scatter.7.cloned.1.call-done = bf16[256,256]{1,0:T(8,128)(2,1)} async-done(((bf16[256,2048]{1,0:T(8,128)(2,1)}), bf16[256,256]{1,0:T(8,128)(2,1)}) %reduce-scatter.7.cloned.1.call-update) | async-done | bytes 131088 | tf_op jit(solution)/shard_map/reduce_scatter | solution.py:148
  837.1 85.7 %reduce-scatter.11.cloned.1.call-done = bf16[256,256]{1,0:T(8,128)(2,1)} async-done(((bf16[256,2048]{1,0:T(8,128)(2,1)}), bf16[256,256]{1,0:T(8,128)(2,1)}) %reduce-scatter.11.cloned.1.call-update) | async-done | bytes 131088 | tf_op jit(solution)/shard_map/reduce_scatter | solution.py:148
  (103 shorter events, 21.4 us)
Async XLA Ops:
  7.2 737.0 %copy-start = (bf16[704,2048]{1,0:T(8,128)(2,1)S(1)}, bf16[704,2048]{1,0:T(8,128)(2,1)}, u32[]{:S(2)}) copy-start(bf16[704,2048]{1,0:T(8,128)(2,1)} %param.31) | copy-start | bytes 8650756
  8.6 46.0 %all-to-all-start = ((s32[32,1,256]{2,1,0:T(1,128)}), s32[32,1,256]{2,1,0:T(1,128)S(1)}, u32[]{:S(2)}, u32[]{:S(2)}) async-start(s32[32,1,256]{2,1,0:T(1,128)} %stack.2), calls=%async_computation | async-start | bytes 65536 | tf_op jit(solution)/shard_map/all_to_all | solution.py:92
  17.8 180.7 %reduce-scatter.9.cloned.1.call-start = ((), (), s32[]{:S(2)}) async-start(), calls=%async_computation.8 | async-start | bytes 4325376 | tf_op jit(solution)/shard_map/reduce_scatter | solution.py:102
  61.0 289.8 %reduce-scatter.5.cloned.1.call-start = ((), (), s32[]{:S(2)}) async-start(), calls=%async_computation.5 | async-start | bytes 4325376 | tf_op jit(solution)/shard_map/reduce_scatter | solution.py:99
  67.4 283.6 %copy-start.6 = (bf16[2048,64]{0,1:T(8,128)(2,1)S(1)}, bf16[2048,64]{0,1:T(8,128)(2,1)}, u32[]{:S(2)}) copy-start(bf16[2048,64]{0,1:T(8,128)(2,1)} %param.32) | copy-start | bytes 786436
  67.4 286.4 %copy-start.16 = (s32[32]{0:T(128)S(1)}, s32[32]{0:T(128)}, u32[]{:S(2)}) copy-start(s32[32]{0:T(128)} %param.20) | copy-start | bytes 388
  67.4 287.0 %copy-start.17 = (s32[32]{0:T(128)S(1)}, s32[32]{0:T(128)}, u32[]{:S(2)}) copy-start(s32[32]{0:T(128)} %param.21) | copy-start | bytes 388
  67.4 424.9 %copy-start.14 = (f32[2048]{0:T(1024)S(1)}, f32[2048]{0:T(1024)}, u32[]{:S(2)}) copy-start(f32[2048]{0:T(1024)} %param.23) | copy-start | bytes 24580
  67.4 363.5 %all-gather.6.cloned.1.call-start = ((), (), s32[]{:S(2)}) async-start(), calls=%async_computation.9 | async-start | bytes 1179648 | tf_op jit(solution)/shard_map/all_gather | solution.py:112
  198.5 292.1 %all-gather.4.cloned.1.call-start = ((), (), s32[]{:S(2)}) async-start(), calls=%async_computation.6 | async-start | bytes 1179648 | tf_op jit(solution)/shard_map/all_gather | solution.py:112
  350.9 388.1 %all-reduce.3.cloned.1.call-start = ((), (), s32[]{:S(2)}) async-start(), calls=%async_computation.11 | async-start | bytes 4194304 | tf_op jit(solution)/shard_map/psum | solution.py:140
  351.6 145.1 %collective-permute-start.1 = (bf16[1792,64]{0,1:T(8,128)(2,1)}, bf16[1792,64]{0,1:T(8,128)(2,1)S(1)}, u32[]{:S(2)}, u32[]{:S(2)}) collective-permute-start(bf16[1792,64]{0,1:T(8,128)(2,1)} %slice.35), channel_id=1, source_target_pairs={{0,8},{8,0},{16,24},{24,16},{32,40},{40,32},{48,56},{56,48},{64,72... | collective-permute-start | bytes 688136 | tf_op jit(solution)/shard_map/ppermute | solution.py:12
  353.3 180.8 %collective-permute-start = (bf16[1792,64]{0,1:T(8,128)(2,1)}, bf16[1792,64]{0,1:T(8,128)(2,1)}, u32[]{:S(2)}, u32[]{:S(2)}) collective-permute-start(bf16[1792,64]{0,1:T(8,128)(2,1)} %slice.33), channel_id=1, source_target_pairs={{0,8},{8,0},{16,24},{24,16},{32,40},{40,32},{48,56},{56,48},{64,72... | collective-permute-start | bytes 688136 | tf_op jit(solution)/shard_map/ppermute | solution.py:12
  504.9 29.3 %slice-start = ((s8[16777216]{0:T(1024)(128)(4,1)}), s8[4194304]{0:T(1024)(128)(4,1)S(1)}, s32[]{:S(2)}) async-start(s8[16777216]{0:T(1024)(128)(4,1)} %bitcast.173), calls=%async_computation.12 | async-start | bytes 8388608
  504.9 29.3 %slice-start.1 = ((s8[16777216]{0:T(1024)(128)(4,1)}), s8[4194304]{0:T(1024)(128)(4,1)S(1)}, s32[]{:S(2)}) async-start(s8[16777216]{0:T(1024)(128)(4,1)} %bitcast.173), calls=%async_computation.13 | async-start | bytes 8388608
  504.9 29.3 %slice-start.2 = ((s8[16777216]{0:T(1024)(128)(4,1)}), s8[4194304]{0:T(1024)(128)(4,1)S(1)}, s32[]{:S(2)}) async-start(s8[16777216]{0:T(1024)(128)(4,1)} %bitcast.173), calls=%async_computation.14 | async-start | bytes 8388608
  519.4 14.2 %copy-start.13 = (bf16[2048,64]{0,1:T(8,128)(2,1)S(1)}, bf16[2048,64]{0,1:T(8,128)(2,1)}, u32[]{:S(2)}) copy-start(bf16[2048,64]{0,1:T(8,128)(2,1)} %param.26) | copy-start | bytes 786436
  519.4 14.8 %slice-start.3 = ((s8[16777216]{0:T(1024)(128)(4,1)}), s8[4194304]{0:T(1024)(128)(4,1)S(1)}, s32[]{:S(2)}) async-start(s8[16777216]{0:T(1024)(128)(4,1)} %bitcast.173), calls=%async_computation.15 | async-start | bytes 8388608
  519.4 14.8 %copy-start.7 = (bf16[2048,64]{0,1:T(8,128)(2,1)S(1)}, bf16[2048,64]{0,1:T(8,128)(2,1)}, u32[]{:S(2)}) copy-start(bf16[2048,64]{0,1:T(8,128)(2,1)} %param.33) | copy-start | bytes 786436
  533.6 8.1 slice-start.4
  534.2 7.5 slice-start.5
  548.3 193.9 %copy-start.15 = (f32[2048]{0:T(1024)S(1)}, f32[2048]{0:T(1024)}, u32[]{:S(2)}) copy-start(f32[2048]{0:T(1024)} %param.28) | copy-start | bytes 24580
  548.3 287.1 %reduce-scatter.7.cloned.1.call-start = ((), (), s32[]{:S(2)}) async-start(), calls=%async_computation.7 | async-start | bytes 1179648 | tf_op jit(solution)/shard_map/reduce_scatter | solution.py:148
  750.8 171.9 %reduce-scatter.11.cloned.1.call-start = ((), (), s32[]{:S(2)}) async-start(), calls=%async_computation.10 | async-start | bytes 1179648 | tf_op jit(solution)/shard_map/reduce_scatter | solution.py:148
  (12 other events, 44.0 us)
Sparse Core Ops, SparseCore 0:
  61.1 137.3 reduce-scatter.8
  201.0 149.7 reduce-scatter.4
  353.3 77.5 all-gather.5
  433.3 57.3 all-gather.3
  548.4 190.5 all-reduce.2
  750.9 84.4 reduce-scatter.6
  839.9 82.8 reduce-scatter.10
